TPU v7x, 32 devices: a whole 2x2x4 slice. The times are simulated.
32 devices in a mesh: gx: 8 (over z, x), gy: 4 (over y, core).
Axes of the slice: x: 2, y: 2, z: 4, core: 2. Of those that a mesh axis runs over, the one named last changes fastest.
Arguments:
- patches: bfloat16 [128, 64, 256], P('gx', 'gy'), may hold values from -9 to 9
- w_query: bfloat16 [256, 256], replicated, may hold values from -2 to 2
- w_key: bfloat16 [256, 256], replicated, may hold values from -2 to 2
- w_value: bfloat16 [256, 256], replicated, may hold values from -0.375 to 0.375
- w_out: bfloat16 [256, 256], replicated, may hold values from -0.375 to 0.375
- region_memory: bfloat16 [8, 4, 4, 64, 512], P('gx', 'gy'), may hold values from -6 to 6
- region_owner: int32 [8, 4, 4, 2], P('gx', 'gy'), may hold values from 0 to 7, all different within a row; in each aligned block of 4 rows (0 to 3, 4 to 7, ..., all dimensions but the last counted through in order) at most 2 rows name the same one
- region_local: int32 [8, 4, 4, 2], P('gx', 'gy'), may hold values from 0 to 3
- grad_out: bfloat16 [128, 64, 256], P('gx', 'gy'), may hold values from -6 to 6
Outputs:
- layer_out: bfloat16 [128, 64, 256], P('gx', 'gy')
- grad_patches: bfloat16 [128, 64, 256], P('gx', 'gy')
- grad_w_query: float32 [256, 256], replicated
- grad_w_key: float32 [256, 256], replicated
- grad_w_value: float32 [256, 256], replicated
- grad_w_out: float32 [256, 256], replicated
Inputs may be any that keep to these rules, and one draw needn't show every extreme that they name: `region_owner`: each block names two different owner tiles. The blocks of one tile name one owner at most 2 times, a bound that some tile reaches.
All inputs are finite; a program needn't handle non-finite values.
Results may differ from a plain program's by a relative error of at most 0.02.
Values may be sent and summed in bfloat16 or wider, within the bound.
No kernel may reach another device: no remote copies, remote signals or barrier semaphores. Data moves between devices by JAX's collectives and lax.ppermute only.
A program may use at most 64 MiB of HBM per device.

v0:
```python
import math
import jax
import jax.numpy as jnp
from jax import lax
from jax.sharding import PartitionSpec as P

D = 256
HEADS = 2
HEAD_DIM = 128
BSIDE = 8
BT = 64
masked_score = -1000000000.0


def padded(block, sides, width):
    for axis, dim in sides:
        count = lax.axis_size(axis)
        forward = [(i, i + 1) for i in range(count - 1)]
        backward = [(target, source) for source, target in forward]
        low = lax.ppermute(
            lax.slice_in_dim(block, block.shape[dim] - width, None, axis=dim), axis, forward
        )
        high = lax.ppermute(lax.slice_in_dim(block, 0, width, axis=dim), axis, backward)
        block = jnp.concatenate([low, block, high], axis=dim)
    return block


def to_blocks(grid_array):
    grid_rows, grid_cols, feature_width = grid_array.shape
    shaped = grid_array.reshape(grid_rows // BSIDE, BSIDE, grid_cols // BSIDE, BSIDE, feature_width)
    return shaped.transpose(0, 2, 1, 3, 4).reshape(
        grid_rows // BSIDE, grid_cols // BSIDE, BSIDE * BSIDE, feature_width
    )


def from_blocks(block_array):
    block_rows, block_cols, block_tokens, feature_width = block_array.shape
    shaped = block_array.reshape(block_rows, block_cols, BSIDE, BSIDE, feature_width)
    return shaped.transpose(0, 2, 1, 3, 4).reshape(
        block_rows * BSIDE, block_cols * BSIDE, feature_width
    )


def split_heads(source):
    return source.reshape(source.shape[:-1] + (HEADS, source.shape[-1] // HEADS))


def key_pieces(keyval_pad, key_valid, region_keyval):
    block_rows, block_cols = (region_keyval.shape[0], region_keyval.shape[1])
    pieces = []
    for row_off in range(3):
        for col_off in range(3):
            key_block = keyval_pad[row_off : row_off + block_rows, col_off : col_off + block_cols]
            valid_mask = key_valid[row_off : row_off + block_rows, col_off : col_off + block_cols]
            pieces.append((key_block[..., :D], key_block[..., D:], valid_mask))
    merged = region_keyval.reshape(block_rows, block_cols, 2 * BT, 2 * D)
    pieces.append(
        (merged[..., :D], merged[..., D:], jnp.ones((block_rows, block_cols), dtype=jnp.bool_))
    )
    return pieces


def piece_scores(query_heads, key_part, valid_mask):
    scores = jnp.einsum(
        "abqhe,abkhe->abhqk", query_heads, split_heads(key_part), preferred_element_type=jnp.float32
    )
    scores = scores * (1.0 / math.sqrt(HEAD_DIM))
    return jnp.where(valid_mask[:, :, None, None, None], scores, masked_score)


def attend_forward(query_blocks, keyval_pad, key_valid, region_keyval):
    query_heads = split_heads(query_blocks)
    pieces = key_pieces(keyval_pad, key_valid, region_keyval)
    scores = [
        piece_scores(query_heads, key_part, valid_mask)
        for key_part, value_part, valid_mask in pieces
    ]
    row_top = jnp.max(jnp.concatenate(scores, -1), -1, keepdims=True)
    row_total = sum(
        (jnp.sum(jnp.exp(part_scores - row_top), -1, keepdims=True) for part_scores in scores)
    )
    log_total = row_top + jnp.log(row_total)
    mixed_sum = jnp.zeros(query_heads.shape, jnp.float32)
    for part_scores, (key_part, value_part, valid_mask) in zip(scores, pieces):
        weights = jnp.exp(part_scores - log_total).astype(jnp.bfloat16)
        mixed_sum = mixed_sum + jnp.einsum(
            "abhqk,abkhe->abqhe",
            weights,
            split_heads(value_part),
            preferred_element_type=jnp.float32,
        )
    output = mixed_sum.reshape(query_blocks.shape).astype(jnp.bfloat16)
    return (output, log_total[..., 0])


def query_grads(
    query_blocks, keyval_pad, key_valid, region_keyval, log_total, dout_blocks, delta_rows
):
    query_heads = split_heads(query_blocks)
    dout_heads = split_heads(dout_blocks)
    accum_sum = jnp.zeros(query_heads.shape, jnp.float32)
    for key_part, value_part, valid_mask in key_pieces(keyval_pad, key_valid, region_keyval):
        part_scores = piece_scores(query_heads, key_part, valid_mask)
        prob_part = jnp.exp(part_scores - log_total[..., None])
        grad_prob = jnp.einsum(
            "abqhe,abkhe->abhqk",
            dout_heads,
            split_heads(value_part),
            preferred_element_type=jnp.float32,
        )
        grad_score = (prob_part * (grad_prob - delta_rows[..., None])).astype(jnp.bfloat16)
        accum_sum = accum_sum + jnp.einsum(
            "abhqk,abkhe->abqhe",
            grad_score,
            split_heads(key_part),
            preferred_element_type=jnp.float32,
        )
    return (
        (accum_sum * (1.0 / math.sqrt(HEAD_DIM))).reshape(query_blocks.shape).astype(jnp.bfloat16)
    )


def key_grads(keyval_center, query_pad, dout_pad, log_pad, delta_pad, query_valid):
    block_rows, block_cols = (keyval_center.shape[0], keyval_center.shape[1])
    key_heads = split_heads(keyval_center[..., :D])
    value_heads = split_heads(keyval_center[..., D:])
    grad_key = jnp.zeros(key_heads.shape, jnp.float32)
    grad_value = jnp.zeros(key_heads.shape, jnp.float32)
    for row_off in range(3):
        for col_off in range(3):
            query_heads = split_heads(
                query_pad[row_off : row_off + block_rows, col_off : col_off + block_cols]
            )
            dout_heads = split_heads(
                dout_pad[row_off : row_off + block_rows, col_off : col_off + block_cols]
            )
            log_part = log_pad[row_off : row_off + block_rows, col_off : col_off + block_cols]
            delta_part = delta_pad[row_off : row_off + block_rows, col_off : col_off + block_cols]
            valid_mask = query_valid[row_off : row_off + block_rows, col_off : col_off + block_cols]
            part_scores = jnp.einsum(
                "abqhe,abkhe->abhqk", query_heads, key_heads, preferred_element_type=jnp.float32
            )
            part_scores = part_scores * (1.0 / math.sqrt(HEAD_DIM))
            prob_part = jnp.where(
                valid_mask[:, :, None, None, None], jnp.exp(part_scores - log_part[..., None]), 0.0
            )
            grad_prob = jnp.einsum(
                "abqhe,abkhe->abhqk", dout_heads, value_heads, preferred_element_type=jnp.float32
            )
            grad_score = (prob_part * (grad_prob - delta_part[..., None])).astype(jnp.bfloat16)
            grad_key = grad_key + jnp.einsum(
                "abhqk,abqhe->abkhe", grad_score, query_heads, preferred_element_type=jnp.float32
            )
            rounded_prob = prob_part.astype(jnp.bfloat16)
            grad_value = grad_value + jnp.einsum(
                "abhqk,abqhe->abkhe", rounded_prob, dout_heads, preferred_element_type=jnp.float32
            )
    out_shape = (block_rows, block_cols, BT, D)
    grad_key = (grad_key * (1.0 / math.sqrt(HEAD_DIM))).reshape(out_shape).astype(jnp.bfloat16)
    return (grad_key, grad_value.reshape(out_shape).astype(jnp.bfloat16))


def inner_rows(left_rows, right_rows):
    return lax.dot_general(
        left_rows, right_rows, (((0,), (0,)), ((), ())), preferred_element_type=jnp.float32
    )


def on_device(
    patches, w_query, w_key, w_value, w_out, region_memory, region_owner, region_local, grad_out
):
    tile_rows, tile_cols, model_width = patches.shape
    block_rows, block_cols = (tile_rows // BSIDE, tile_cols // BSIDE)
    block_count = block_rows * block_cols
    flat_in = patches.reshape(-1, model_width)
    w_pair = jnp.concatenate([w_key, w_value], 1)
    queries = jnp.dot(flat_in, w_query, preferred_element_type=jnp.float32).astype(jnp.bfloat16)
    keyvals = jnp.dot(flat_in, w_pair, preferred_element_type=jnp.float32).astype(jnp.bfloat16)
    keyvals = keyvals.reshape(tile_rows, tile_cols, 2 * model_width)
    keyval_grid = padded(keyvals, (("gx", 0), ("gy", 1)), BSIDE)
    keyval_pad = to_blocks(keyval_grid)
    gx_count = lax.axis_size("gx")
    gy_count = lax.axis_size("gy")
    row_ids = lax.axis_index("gx") * block_rows - 1 + jnp.arange(block_rows + 2, dtype=jnp.int32)
    col_ids = lax.axis_index("gy") * block_cols - 1 + jnp.arange(block_cols + 2, dtype=jnp.int32)
    row_valid = (row_ids >= 0) & (row_ids < block_rows * gx_count)
    col_valid = (col_ids >= 0) & (col_ids < block_cols * gy_count)
    key_valid = row_valid[:, None] & col_valid[None, :]
    owners = region_owner.reshape(2 * block_count)
    local_ids = region_local.reshape(2 * block_count)
    memory_local = region_memory.reshape(
        region_memory.shape[2], region_memory.shape[3], region_memory.shape[4]
    )
    region_count = memory_local.shape[0]
    row_tables = lax.all_gather(memory_local, "gx", axis=0, tiled=True)
    fetched = jnp.take(row_tables, owners * region_count + local_ids, axis=0)
    region_keyval = fetched.reshape(
        block_rows, block_cols, 2, memory_local.shape[1], memory_local.shape[2]
    )
    query_blocks = to_blocks(queries.reshape(tile_rows, tile_cols, model_width))
    outputs, log_totals = attend_forward(query_blocks, keyval_pad, key_valid, region_keyval)
    attended = from_blocks(outputs).reshape(-1, model_width)
    layer_out = jnp.dot(attended, w_out, preferred_element_type=jnp.float32).astype(jnp.bfloat16)
    grad_flat = grad_out.reshape(-1, model_width)
    d_attended = jnp.dot(grad_flat, w_out.T, preferred_element_type=jnp.float32).astype(
        jnp.bfloat16
    )
    grad_out_local = inner_rows(attended, grad_flat)
    dout_blocks = to_blocks(d_attended.reshape(tile_rows, tile_cols, model_width))
    delta_rows = jnp.sum(
        split_heads(dout_blocks).astype(jnp.float32) * split_heads(outputs).astype(jnp.float32), -1
    )
    delta_rows = delta_rows.transpose(0, 1, 3, 2)
    d_queries = query_grads(
        query_blocks, keyval_pad, key_valid, region_keyval, log_totals, dout_blocks, delta_rows
    )
    query_grid = jnp.concatenate(
        [
            queries.reshape(tile_rows, tile_cols, model_width),
            d_attended.reshape(tile_rows, tile_cols, model_width),
        ],
        -1,
    )
    query_halo = padded(query_grid, (("gx", 0), ("gy", 1)), BSIDE)
    stat_grid = from_blocks(jnp.concatenate([log_totals, delta_rows], 2).transpose(0, 1, 3, 2))
    stat_halo = padded(stat_grid, (("gx", 0), ("gy", 1)), BSIDE)
    query_all = to_blocks(query_halo)
    stat_pad = to_blocks(stat_halo).transpose(0, 1, 3, 2)
    d_keys, d_values = key_grads(
        keyval_pad[1:-1, 1:-1],
        query_all[..., :model_width],
        query_all[..., model_width:],
        stat_pad[:, :, :HEADS],
        stat_pad[:, :, HEADS:],
        key_valid,
    )
    dq_flat = from_blocks(d_queries).reshape(-1, model_width)
    dk_flat = from_blocks(d_keys).reshape(-1, model_width)
    dv_flat = from_blocks(d_values).reshape(-1, model_width)
    grads_joined = jnp.concatenate([dq_flat, dk_flat, dv_flat], 1)
    w_stacked = jnp.concatenate([w_query.T, w_key.T, w_value.T], 0)
    grad_patches = jnp.dot(grads_joined, w_stacked, preferred_element_type=jnp.float32).astype(
        jnp.bfloat16
    )
    summed = lax.psum(
        (
            inner_rows(flat_in, dq_flat),
            inner_rows(flat_in, dk_flat),
            inner_rows(flat_in, dv_flat),
            grad_out_local,
        ),
        ("gx", "gy"),
    )
    return (
        layer_out.reshape(tile_rows, tile_cols, model_width),
        grad_patches.reshape(tile_rows, tile_cols, model_width),
        summed[0],
        summed[1],
        summed[2],
        summed[3],
    )


def solution(mesh):
    return jax.shard_map(
        on_device,
        mesh=mesh,
        in_specs=(
            P("gx", "gy", None),
            P(),
            P(),
            P(),
            P(),
            P("gx", "gy", None, None, None),
            P("gx", "gy", None, None),
            P("gx", "gy", None, None),
            P("gx", "gy", None),
        ),
        out_specs=(P("gx", "gy", None), P("gx", "gy", None), P(), P(), P(), P()),
        check_vma=False,
    )
```

profile of v0, /device:TPU:0, one launch (start us, length us, event | category | flops | bytes accessed | tf_op | source)
XLA Modules:
  0.0 271.7 jit_solution(11771590287470757042)
XLA Ops:
  10.6 5.5 %collective-permute-start = (bf16[8,16,512]{2,1,0:T(8,128)(2,1)S(1)}, bf16[8,16,512]{2,1,0:T(8,128)(2,1)S(1)}, u32[]{:S(2)}, u32[]{:S(2)}) collective-permute-start(bf16[8,16,512]{2,1,0:T(8,128)(2,1)S(1)} %bitcast.503), channel_id=1, source_target_pairs={{0,4},{4,8},{8,12},{12,16},{16,20},{20,24},{24,28},{1,5},{5,9},{9,... | collective-permute-start | bytes 393224 | tf_op jit(solution)/shard_map/ppermute | solution.py:20
  18.4 4.8 %collective-permute-start.4 = (bf16[8,16,512]{2,1,0:T(8,128)(2,1)S(1)}, bf16[8,16,512]{2,1,0:T(8,128)(2,1)S(1)}, u32[]{:S(2)}, u32[]{:S(2)}) collective-permute-start(bf16[8,16,512]{2,1,0:T(8,128)(2,1)S(1)} %get-tuple-element.85), channel_id=1, source_target_pairs={{0,4},{4,8},{8,12},{12,16},{16,20},{20,24},{24,28},{1,5},{5,9},{9,... | collective-permute-start | bytes 393224 | tf_op jit(solution)/shard_map/ppermute | solution.py:20
  25.1 3.5 %collective-permute-done.4 = bf16[8,16,512]{2,1,0:T(8,128)(2,1)S(1)} collective-permute-done((bf16[8,16,512]{2,1,0:T(8,128)(2,1)S(1)}, bf16[8,16,512]{2,1,0:T(8,128)(2,1)S(1)}, u32[]{:S(2)}, u32[]{:S(2)}) %collective-permute-start.4) | collective-permute-done | bytes 131104 | tf_op jit(solution)/shard_map/ppermute | solution.py:20
  28.6 1.5 collective-permute-done.5
  33.0 4.8 %collective-permute-start.2 = (bf16[32,8,512]{2,1,0:T(8,128)(2,1)S(1)}, bf16[32,8,512]{2,1,0:T(8,128)(2,1)S(1)}, u32[]{:S(2)}, u32[]{:S(2)}) collective-permute-start(bf16[32,8,512]{2,1,0:T(8,128)(2,1)S(1)} %get-tuple-element.83), channel_id=1, source_target_pairs={{0,1},{1,2},{2,3},{4,5},{5,6},{6,7},{8,9},{9,10},{10,11},{12,13},{... | collective-permute-start | bytes 786440 | tf_op jit(solution)/shard_map/ppermute | solution.py:20
  39.7 2.8 %collective-permute-done.3 = bf16[32,8,512]{2,1,0:T(8,128)(2,1)} collective-permute-done((bf16[32,8,512]{2,1,0:T(8,128)(2,1)S(1)}, bf16[32,8,512]{2,1,0:T(8,128)(2,1)}, u32[]{:S(2)}, u32[]{:S(2)}) %collective-permute-start.3) | collective-permute-done | bytes 262176 | tf_op jit(solution)/shard_map/ppermute | solution.py:23
  50.2 1.5 slice_bitcast_fusion
  51.7 13.7 %all-gather.3.cloned.1.call-done = bf16[1,1,32,64,512]{4,3,1,0,2:T(8,128)(2,1)} async-done(((bf16[1,1,4,64,512]{4,3,1,0,2:T(8,128)(2,1)}), bf16[1,1,32,64,512]{4,3,1,0,2:T(8,128)(2,1)}) %all-gather.3.cloned.1.call-update) | async-done | bytes 2097168 | tf_op jit(solution)/shard_map/all_gather | solution.py:195
  65.4 2.2 gather_fusion
  75.2 2.1 fusion.84
  77.3 2.2 convolution_add_fusion.24
  79.5 2.2 convolution_add_fusion.23
  88.7 2.4 collective-permute-start.8
  94.3 4.7 %collective-permute-done.9 = f32[8,16,4]{1,0,2:T(8,128)S(1)} collective-permute-done((f32[8,16,4]{1,0,2:T(8,128)S(1)}, f32[8,16,4]{1,0,2:T(8,128)S(1)}, u32[]{:S(2)}, u32[]{:S(2)}) %collective-permute-start.9) | collective-permute-done | bytes 2080 | tf_op jit(solution)/shard_map/ppermute | solution.py:23
  100.3 1.5 collective-permute-start.11
  102.8 2.4 collective-permute-done.11
  111.9 1.6 convert_element_type.219
  113.5 1.6 copy.530
  115.1 2.0 convolution_add_fusion.15
  127.3 130.5 %all-reduce.3.cloned.1.call-done = (f32[256,256]{0,1:T(8,128)}, f32[256,256]{0,1:T(8,128)}, f32[256,256]{0,1:T(8,128)}, f32[256,256]{1,0:T(8,128)}) async-done(((f32[256,256]{0,1:T(8,128)}, f32[256,256]{0,1:T(8,128)}, f32[256,256]{0,1:T(8,128)}, f32[256,256]{1,0:T(8,128)}), (f32[256,256]{0,1:T(8,128)}, f32[256,256]{0,1:T(8,128)}, f32[256,256]{0,1:T(8,128)}, ...) | async-done | bytes 1048592 | tf_op jit(solution)/shard_map/psum | solution.py:245
  257.8 1.8 copy.531
  259.6 1.8 copy.532
  261.4 1.8 copy.533
  263.2 1.7 copy.1109
  (302 shorter events, 55.3 us)
Async XLA Ops:
  7.2 17.4 %copy-start.59 = (s32[1,1,4,2]{2,3,1,0:T(2,128)S(1)}, s32[1,1,4,2]{2,3,1,0:T(2,128)}, u32[]{:S(2)}) copy-start(s32[1,1,4,2]{2,3,1,0:T(2,128)} %param.16) | copy-start | bytes 100
  7.2 58.2 %all-gather.3.cloned.1.call-start = ((), (), s32[]{:S(2)}) async-start(), calls=%async_computation | async-start | bytes 2359296 | tf_op jit(solution)/shard_map/all_gather | solution.py:195
  7.9 249.9 %all-reduce.3.cloned.1.call-start = ((), (), s32[]{:S(2)}) async-start(), calls=%async_computation.1 | async-start | bytes 2097152 | tf_op jit(solution)/shard_map/psum | solution.py:245
  9.3 23.5 %collective-permute-start.1 = (bf16[8,16,512]{2,1,0:T(8,128)(2,1)S(1)}, bf16[8,16,512]{2,1,0:T(8,128)(2,1)S(1)}, u32[]{:S(2)}, u32[]{:S(2)}) collective-permute-start(bf16[8,16,512]{2,1,0:T(8,128)(2,1)S(1)} %bitcast.504), channel_id=1, source_target_pairs={{4,0},{8,4},{12,8},{16,12},{20,16},{24,20},{28,24},{5,1},{9,5},{13... | collective-permute-start | bytes 393224 | tf_op jit(solution)/shard_map/ppermute | solution.py:23
  10.6 22.2 %collective-permute-start = (bf16[8,16,512]{2,1,0:T(8,128)(2,1)S(1)}, bf16[8,16,512]{2,1,0:T(8,128)(2,1)S(1)}, u32[]{:S(2)}, u32[]{:S(2)}) collective-permute-start(bf16[8,16,512]{2,1,0:T(8,128)(2,1)S(1)} %bitcast.503), channel_id=1, source_target_pairs={{0,4},{4,8},{8,12},{12,16},{16,20},{20,24},{24,28},{1,5},{5,9},{9,... | collective-permute-start | bytes 393224 | tf_op jit(solution)/shard_map/ppermute | solution.py:20
  18.4 10.2 %collective-permute-start.4 = (bf16[8,16,512]{2,1,0:T(8,128)(2,1)S(1)}, bf16[8,16,512]{2,1,0:T(8,128)(2,1)S(1)}, u32[]{:S(2)}, u32[]{:S(2)}) collective-permute-start(bf16[8,16,512]{2,1,0:T(8,128)(2,1)S(1)} %get-tuple-element.85), channel_id=1, source_target_pairs={{0,4},{4,8},{8,12},{12,16},{16,20},{20,24},{24,28},{1,5},{5,9},{9,... | collective-permute-start | bytes 393224 | tf_op jit(solution)/shard_map/ppermute | solution.py:20
  23.2 6.9 %collective-permute-start.5 = (bf16[8,16,512]{2,1,0:T(8,128)(2,1)S(1)}, bf16[8,16,512]{2,1,0:T(8,128)(2,1)S(1)}, u32[]{:S(2)}, u32[]{:S(2)}) collective-permute-start(bf16[8,16,512]{2,1,0:T(8,128)(2,1)S(1)} %get-tuple-element.86), channel_id=1, source_target_pairs={{4,0},{8,4},{12,8},{16,12},{20,16},{24,20},{28,24},{5,1},{9,5},{13... | collective-permute-start | bytes 393224 | tf_op jit(solution)/shard_map/ppermute | solution.py:23
  25.0 20.0 %copy-start.75 = (pred[2,2]{1,0:T(4,128)(4,1)}, pred[2,2]{1,0:T(4,128)(4,1)S(1)}, u32[]{:S(2)}) copy-start(pred[2,2]{1,0:T(4,128)(4,1)S(1)} %get-tuple-element.112) | copy-start | bytes 16
  25.0 20.3 %copy-start.73 = (pred[2,2]{1,0:T(4,128)(4,1)}, pred[2,2]{1,0:T(4,128)(4,1)S(1)}, u32[]{:S(2)}) copy-start(pred[2,2]{1,0:T(4,128)(4,1)S(1)} %get-tuple-element.113) | copy-start | bytes 16
  25.0 20.5 %copy-start.71 = (pred[2,2]{1,0:T(4,128)(4,1)}, pred[2,2]{1,0:T(4,128)(4,1)S(1)}, u32[]{:S(2)}) copy-start(pred[2,2]{1,0:T(4,128)(4,1)S(1)} %get-tuple-element.114) | copy-start | bytes 16
  25.0 20.7 %copy-start.69 = (pred[2,2]{1,0:T(4,128)(4,1)}, pred[2,2]{1,0:T(4,128)(4,1)S(1)}, u32[]{:S(2)}) copy-start(pred[2,2]{1,0:T(4,128)(4,1)S(1)} %get-tuple-element.115) | copy-start | bytes 16
  25.0 20.9 %copy-start.65 = (pred[2,2]{1,0:T(4,128)(4,1)}, pred[2,2]{1,0:T(4,128)(4,1)S(1)}, u32[]{:S(2)}) copy-start(pred[2,2]{1,0:T(4,128)(4,1)S(1)} %get-tuple-element.117) | copy-start | bytes 16
  25.0 21.8 %copy-start.63 = (pred[2,2]{1,0:T(4,128)(4,1)}, pred[2,2]{1,0:T(4,128)(4,1)S(1)}, u32[]{:S(2)}) copy-start(pred[2,2]{1,0:T(4,128)(4,1)S(1)} %get-tuple-element.118) | copy-start | bytes 16
  25.1 22.6 %copy-start.61 = (pred[2,2]{1,0:T(4,128)(4,1)}, pred[2,2]{1,0:T(4,128)(4,1)S(1)}, u32[]{:S(2)}) copy-start(pred[2,2]{1,0:T(4,128)(4,1)S(1)} %get-tuple-element.111) | copy-start | bytes 16
  25.1 23.4 %copy-start.77 = (pred[2,2]{1,0:T(4,128)(4,1)}, pred[2,2]{1,0:T(4,128)(4,1)S(1)}, u32[]{:S(2)}) copy-start(pred[2,2]{1,0:T(4,128)(4,1)S(1)} %get-tuple-element.119) | copy-start | bytes 16
  25.1 24.3 %copy-start.67 = (pred[2,2]{1,0:T(4,128)(4,1)}, pred[2,2]{1,0:T(4,128)(4,1)S(1)}, u32[]{:S(2)}) copy-start(pred[2,2]{1,0:T(4,128)(4,1)S(1)} %get-tuple-element.116) | copy-start | bytes 16
  30.2 9.3 %collective-permute-start.6 = (bf16[32,8,512]{2,1,0:T(8,128)(2,1)S(1)}, bf16[32,8,512]{2,1,0:T(8,128)(2,1)S(1)}, u32[]{:S(2)}, u32[]{:S(2)}) collective-permute-start(bf16[32,8,512]{2,1,0:T(8,128)(2,1)S(1)} %get-tuple-element.79), channel_id=1, source_target_pairs={{0,1},{1,2},{2,3},{4,5},{5,6},{6,7},{8,9},{9,10},{10,11},{12,13},{... | collective-permute-start | bytes 786440 | tf_op jit(solution)/shard_map/ppermute | solution.py:20
  31.5 8.0 %collective-permute-start.7 = (bf16[32,8,512]{2,1,0:T(8,128)(2,1)S(1)}, bf16[32,8,512]{2,1,0:T(8,128)(2,1)S(1)}, u32[]{:S(2)}, u32[]{:S(2)}) collective-permute-start(bf16[32,8,512]{2,1,0:T(8,128)(2,1)S(1)} %get-tuple-element.80), channel_id=1, source_target_pairs={{1,0},{2,1},{3,2},{5,4},{6,5},{7,6},{9,8},{10,9},{11,10},{13,12},{... | collective-permute-start | bytes 786440 | tf_op jit(solution)/shard_map/ppermute | solution.py:23
  33.0 6.8 %collective-permute-start.2 = (bf16[32,8,512]{2,1,0:T(8,128)(2,1)S(1)}, bf16[32,8,512]{2,1,0:T(8,128)(2,1)S(1)}, u32[]{:S(2)}, u32[]{:S(2)}) collective-permute-start(bf16[32,8,512]{2,1,0:T(8,128)(2,1)S(1)} %get-tuple-element.83), channel_id=1, source_target_pairs={{0,1},{1,2},{2,3},{4,5},{5,6},{6,7},{8,9},{9,10},{10,11},{12,13},{... | collective-permute-start | bytes 786440 | tf_op jit(solution)/shard_map/ppermute | solution.py:20
  37.7 4.8 %collective-permute-start.3 = (bf16[32,8,512]{2,1,0:T(8,128)(2,1)S(1)}, bf16[32,8,512]{2,1,0:T(8,128)(2,1)}, u32[]{:S(2)}, u32[]{:S(2)}) collective-permute-start(bf16[32,8,512]{2,1,0:T(8,128)(2,1)S(1)} %get-tuple-element.84), channel_id=1, source_target_pairs={{1,0},{2,1},{3,2},{5,4},{6,5},{7,6},{9,8},{10,9},{11,10},{13,12},{... | collective-permute-start | bytes 786440 | tf_op jit(solution)/shard_map/ppermute | solution.py:23
  88.7 5.5 %collective-permute-start.8 = (f32[8,16,4]{1,0,2:T(8,128)S(1)}, f32[8,16,4]{1,0,2:T(8,128)S(1)}, u32[]{:S(2)}, u32[]{:S(2)}) collective-permute-start(f32[8,16,4]{1,0,2:T(8,128)S(1)} %slice.401), channel_id=1, source_target_pairs={{0,4},{4,8},{8,12},{12,16},{16,20},{20,24},{24,28},{1,5},{5,9},{9,... | collective-permute-start | bytes 6152 | tf_op jit(solution)/shard_map/ppermute | solution.py:20
  93.0 6.0 %collective-permute-start.9 = (f32[8,16,4]{1,0,2:T(8,128)S(1)}, f32[8,16,4]{1,0,2:T(8,128)S(1)}, u32[]{:S(2)}, u32[]{:S(2)}) collective-permute-start(f32[8,16,4]{1,0,2:T(8,128)S(1)} %slice.403), channel_id=1, source_target_pairs={{4,0},{8,4},{12,8},{16,12},{20,16},{24,20},{28,24},{5,1},{9,5},{13... | collective-permute-start | bytes 6152 | tf_op jit(solution)/shard_map/ppermute | solution.py:23
  99.0 3.7 %collective-permute-start.10 = (f32[32,8,4]{1,0,2:T(8,128)S(1)}, f32[32,8,4]{1,0,2:T(8,128)S(1)}, u32[]{:S(2)}, u32[]{:S(2)}) collective-permute-start(f32[32,8,4]{1,0,2:T(8,128)S(1)} %get-tuple-element.89), channel_id=1, source_target_pairs={{0,1},{1,2},{2,3},{4,5},{5,6},{6,7},{8,9},{9,10},{10,11},{12,13},{... | collective-permute-start | bytes 12296 | tf_op jit(solution)/shard_map/ppermute | solution.py:20
  100.3 4.8 %collective-permute-start.11 = (f32[32,8,4]{1,0,2:T(8,128)S(1)}, f32[32,8,4]{1,0,2:T(8,128)S(1)}, u32[]{:S(2)}, u32[]{:S(2)}) collective-permute-start(f32[32,8,4]{1,0,2:T(8,128)S(1)} %get-tuple-element.90), channel_id=1, source_target_pairs={{1,0},{2,1},{3,2},{5,4},{6,5},{7,6},{9,8},{10,9},{11,10},{13,12},{... | collective-permute-start | bytes 12296 | tf_op jit(solution)/shard_map/ppermute | solution.py:23
  (69 other events, 277.6 us)
Sparse Core Ops, SparseCore 0:
  10.2 55.1 all-gather.2
  125.6 132.2 all-reduce.2
where the time goes:
time: 273 us; the launch traced here: 272 us
  waiting for transfers between devices  160 us (59%)
  matrix products  44.2 us (16%)
  starting transfers between devices  28.1 us (10%)
  local copies, waits for them, and re-layouts  20.5 us (8%)
  between operations  15.9 us (6%)
  other arithmetic  3.19 us (1%)
    psum x1, waiting for transfers between devices, on_device(): lax.psum((inner_rows(flat_in, dq_flat), inner_rows(flat_in, dk_flat), inn...  131 us
    ppermute x6, starting transfers between devices, padded(): lax.ppermute(lax.slice_in_dim(block, block.shape[dim] - width, None, axis...  20.1 us
    all_gather x1, waiting for transfers between devices, on_device(): row_tables = lax.all_gather(memory_local, 'gx', axis=0, tiled=True)  13.7 us
    dot_general x10, matrix products, query_grads(): jnp.einsum('abhqk,abkhe->abqhe', grad_score, split_heads(key_part), prefe...  13.1 us
    ppermute x6, waiting for transfers between devices, padded(): lax.ppermute(lax.slice_in_dim(block, 0, width, axis=dim), axis, backward)  11.4 us
    unnamed x166, local copies, waits for them, and re-layouts  10.8 us
    dot_general x9, matrix products, key_grads(): jnp.einsum('abhqk,abqhe->abkhe', grad_score, query_heads, preferred_eleme...  8.38 us
    ppermute x6, starting transfers between devices, padded(): lax.ppermute(lax.slice_in_dim(block, 0, width, axis=dim), axis, backward)  7.92 us
  transfers between devices with their start and end apart: 14, of which 7 were waited for; matrix products, arithmetic and copies ran while one was open for 7% of the time, Pallas kernels for 0%

commit v1 on v0

--- a/solution.py
+++ b/solution.py
@@ -169,6 +169,12 @@
 def on_device(
     patches, w_query, w_key, w_value, w_out, region_memory, region_owner, region_local, grad_out
 ):
+
+    def keep_up_modes_all(local_x, peer_axis, axis_tag):
+        for dev in (peer_axis, axis_tag):
+            local_x = jax.lax.psum(local_x, dev)
+        return local_x
+
     tile_rows, tile_cols, model_width = patches.shape
     block_rows, block_cols = (tile_rows // BSIDE, tile_cols // BSIDE)
     block_count = block_rows * block_cols
@@ -242,14 +248,15 @@
     grad_patches = jnp.dot(grads_joined, w_stacked, preferred_element_type=jnp.float32).astype(
         jnp.bfloat16
     )
-    summed = lax.psum(
+    summed = keep_up_modes_all(
         (
             inner_rows(flat_in, dq_flat),
             inner_rows(flat_in, dk_flat),
             inner_rows(flat_in, dv_flat),
             grad_out_local,
         ),
-        ("gx", "gy"),
+        "gy",
+        "gx",
     )
     return (
         layer_out.reshape(tile_rows, tile_cols, model_width),

time: 273 us -> 262 us (0.960)
  waiting for transfers between devices: 160 us -> 149 us
    psum x1 -> x2, waiting for transfers between devices: 131 us -> 120 us  [keep_up_modes_all(): local_x = jax.lax.psum(local_x, dev)]
  transfers between devices with their start and end apart: 14 -> 15, of which waited for: 7 -> 8; matrix products, arithmetic and copies ran while one was open for 7% -> 7% of each run, Pallas kernels for 0% -> 0%
where the time goes in v1:
time: 262 us; the launch traced here: 261 us
  waiting for transfers between devices  149 us (57%)
  matrix products  44.2 us (17%)
  starting transfers between devices  28.2 us (11%)
  local copies, waits for them, and re-layouts  20.5 us (8%)
  between operations  15.6 us (6%)
  other arithmetic  3.19 us (1%)
    psum x2, waiting for transfers between devices, keep_up_modes_all(): local_x = jax.lax.psum(local_x, dev)  120 us
    ppermute x6, starting transfers between devices, padded(): lax.ppermute(lax.slice_in_dim(block, block.shape[dim] - width, None, axis...  20.1 us
    all_gather x1, waiting for transfers between devices, on_device(): row_tables = lax.all_gather(memory_local, 'gx', axis=0, tiled=True)  13.6 us
    dot_general x10, matrix products, query_grads(): jnp.einsum('abhqk,abkhe->abqhe', grad_score, split_heads(key_part), prefe...  13.1 us
    ppermute x6, waiting for transfers between devices, padded(): lax.ppermute(lax.slice_in_dim(block, 0, width, axis=dim), axis, backward)  11.4 us
    unnamed x166, local copies, waits for them, and re-layouts  10.8 us
    dot_general x9, matrix products, key_grads(): jnp.einsum('abhqk,abqhe->abkhe', grad_score, query_heads, preferred_eleme...  8.38 us
    ppermute x6, starting transfers between devices, padded(): lax.ppermute(lax.slice_in_dim(block, 0, width, axis=dim), axis, backward)  7.92 us
  transfers between devices with their start and end apart: 15, of which 8 were waited for; matrix products, arithmetic and copies ran while one was open for 7% of the time, Pallas kernels for 0%

profile of v1, /device:TPU:0, one launch (start us, length us, event | category | flops | bytes accessed | tf_op | source)
XLA Modules:
  0.0 261.0 jit_solution(17470101024480476024)
XLA Ops:
  10.6 5.5 %collective-permute-start = (bf16[8,16,512]{2,1,0:T(8,128)(2,1)S(1)}, bf16[8,16,512]{2,1,0:T(8,128)(2,1)S(1)}, u32[]{:S(2)}, u32[]{:S(2)}) collective-permute-start(bf16[8,16,512]{2,1,0:T(8,128)(2,1)S(1)} %bitcast.503), channel_id=1, source_target_pairs={{0,4},{4,8},{8,12},{12,16},{16,20},{20,24},{24,28},{1,5},{5,9},{9,... | collective-permute-start | bytes 393224 | tf_op jit(solution)/shard_map/ppermute | solution.py:20
  18.4 4.8 %collective-permute-start.4 = (bf16[8,16,512]{2,1,0:T(8,128)(2,1)S(1)}, bf16[8,16,512]{2,1,0:T(8,128)(2,1)S(1)}, u32[]{:S(2)}, u32[]{:S(2)}) collective-permute-start(bf16[8,16,512]{2,1,0:T(8,128)(2,1)S(1)} %get-tuple-element.89), channel_id=1, source_target_pairs={{0,4},{4,8},{8,12},{12,16},{16,20},{20,24},{24,28},{1,5},{5,9},{9,... | collective-permute-start | bytes 393224 | tf_op jit(solution)/shard_map/ppermute | solution.py:20
  25.1 3.5 %collective-permute-done.4 = bf16[8,16,512]{2,1,0:T(8,128)(2,1)S(1)} collective-permute-done((bf16[8,16,512]{2,1,0:T(8,128)(2,1)S(1)}, bf16[8,16,512]{2,1,0:T(8,128)(2,1)S(1)}, u32[]{:S(2)}, u32[]{:S(2)}) %collective-permute-start.4) | collective-permute-done | bytes 131104 | tf_op jit(solution)/shard_map/ppermute | solution.py:20
  28.6 1.5 collective-permute-done.5
  33.0 4.8 %collective-permute-start.2 = (bf16[32,8,512]{2,1,0:T(8,128)(2,1)S(1)}, bf16[32,8,512]{2,1,0:T(8,128)(2,1)S(1)}, u32[]{:S(2)}, u32[]{:S(2)}) collective-permute-start(bf16[32,8,512]{2,1,0:T(8,128)(2,1)S(1)} %get-tuple-element.87), channel_id=1, source_target_pairs={{0,1},{1,2},{2,3},{4,5},{5,6},{6,7},{8,9},{9,10},{10,11},{12,13},{... | collective-permute-start | bytes 786440 | tf_op jit(solution)/shard_map/ppermute | solution.py:20
  39.7 2.8 %collective-permute-done.3 = bf16[32,8,512]{2,1,0:T(8,128)(2,1)} collective-permute-done((bf16[32,8,512]{2,1,0:T(8,128)(2,1)S(1)}, bf16[32,8,512]{2,1,0:T(8,128)(2,1)}, u32[]{:S(2)}, u32[]{:S(2)}) %collective-permute-start.3) | collective-permute-done | bytes 262176 | tf_op jit(solution)/shard_map/ppermute | solution.py:23
  50.2 1.5 slice_bitcast_fusion
  51.7 13.6 %all-gather.3.cloned.1.call-done = bf16[1,1,32,64,512]{4,3,1,0,2:T(8,128)(2,1)} async-done(((bf16[1,1,4,64,512]{4,3,1,0,2:T(8,128)(2,1)}), bf16[1,1,32,64,512]{4,3,1,0,2:T(8,128)(2,1)}) %all-gather.3.cloned.1.call-update) | async-done | bytes 2097168 | tf_op jit(solution)/shard_map/all_gather | solution.py:201
  65.4 2.2 gather_fusion
  75.2 2.1 fusion.84
  77.3 2.2 convolution_add_fusion.24
  79.5 2.2 convolution_add_fusion.23
  88.7 2.4 collective-permute-start.8
  94.3 4.7 %collective-permute-done.9 = f32[8,16,4]{1,0,2:T(8,128)S(1)} collective-permute-done((f32[8,16,4]{1,0,2:T(8,128)S(1)}, f32[8,16,4]{1,0,2:T(8,128)S(1)}, u32[]{:S(2)}, u32[]{:S(2)}) %collective-permute-start.9) | collective-permute-done | bytes 2080 | tf_op jit(solution)/shard_map/ppermute | solution.py:23
  102.8 2.4 collective-permute-done.11
  111.9 1.6 convert_element_type.219
  113.5 1.6 copy.530
  115.1 2.0 convolution_add_fusion.15
  125.5 38.2 %all-reduce.7.cloned.1.call-done = (f32[256,256]{0,1:T(8,128)}, f32[256,256]{0,1:T(8,128)}, f32[256,256]{0,1:T(8,128)}, f32[256,256]{1,0:T(8,128)}) async-done(((f32[256,256]{0,1:T(8,128)}, f32[256,256]{0,1:T(8,128)}, f32[256,256]{0,1:T(8,128)}, f32[256,256]{1,0:T(8,128)}), (f32[256,256]{0,1:T(8,128)}, f32[256,256]{0,1:T(8,128)}, f32[256,256]{0,1:T(8,128)}, ...) | async-done | bytes 1048592 | tf_op jit(solution)/shard_map/psum | solution.py:175
  165.6 81.9 %all-reduce.5.cloned.1.call-done = (f32[256,256]{0,1:T(8,128)}, f32[256,256]{0,1:T(8,128)}, f32[256,256]{0,1:T(8,128)}, f32[256,256]{1,0:T(8,128)}) async-done(((f32[256,256]{0,1:T(8,128)}, f32[256,256]{0,1:T(8,128)}, f32[256,256]{0,1:T(8,128)}, f32[256,256]{1,0:T(8,128)}), (f32[256,256]{0,1:T(8,128)}, f32[256,256]{0,1:T(8,128)}, f32[256,256]{0,1:T(8,128)}, ...) | async-done | bytes 1048592 | tf_op jit(solution)/shard_map/psum | solution.py:175
  247.5 1.8 copy.531
  249.3 1.8 copy.532
  251.1 1.8 copy.533
  252.8 1.7 copy.1113
  (305 shorter events, 56.8 us)
Async XLA Ops:
  7.2 58.2 %all-gather.3.cloned.1.call-start = ((), (), s32[]{:S(2)}) async-start(), calls=%async_computation | async-start | bytes 2359296 | tf_op jit(solution)/shard_map/all_gather | solution.py:201
  7.9 155.8 %all-reduce.7.cloned.1.call-start = ((), (), s32[]{:S(2)}) async-start(), calls=%async_computation.2 | async-start | bytes 2097152 | tf_op jit(solution)/shard_map/psum | solution.py:175
  9.3 23.5 %collective-permute-start.1 = (bf16[8,16,512]{2,1,0:T(8,128)(2,1)S(1)}, bf16[8,16,512]{2,1,0:T(8,128)(2,1)S(1)}, u32[]{:S(2)}, u32[]{:S(2)}) collective-permute-start(bf16[8,16,512]{2,1,0:T(8,128)(2,1)S(1)} %bitcast.504), channel_id=1, source_target_pairs={{4,0},{8,4},{12,8},{16,12},{20,16},{24,20},{28,24},{5,1},{9,5},{13... | collective-permute-start | bytes 393224 | tf_op jit(solution)/shard_map/ppermute | solution.py:23
  10.6 22.2 %collective-permute-start = (bf16[8,16,512]{2,1,0:T(8,128)(2,1)S(1)}, bf16[8,16,512]{2,1,0:T(8,128)(2,1)S(1)}, u32[]{:S(2)}, u32[]{:S(2)}) collective-permute-start(bf16[8,16,512]{2,1,0:T(8,128)(2,1)S(1)} %bitcast.503), channel_id=1, source_target_pairs={{0,4},{4,8},{8,12},{12,16},{16,20},{20,24},{24,28},{1,5},{5,9},{9,... | collective-permute-start | bytes 393224 | tf_op jit(solution)/shard_map/ppermute | solution.py:20
  18.4 10.2 %collective-permute-start.4 = (bf16[8,16,512]{2,1,0:T(8,128)(2,1)S(1)}, bf16[8,16,512]{2,1,0:T(8,128)(2,1)S(1)}, u32[]{:S(2)}, u32[]{:S(2)}) collective-permute-start(bf16[8,16,512]{2,1,0:T(8,128)(2,1)S(1)} %get-tuple-element.89), channel_id=1, source_target_pairs={{0,4},{4,8},{8,12},{12,16},{16,20},{20,24},{24,28},{1,5},{5,9},{9,... | collective-permute-start | bytes 393224 | tf_op jit(solution)/shard_map/ppermute | solution.py:20
  23.2 6.9 %collective-permute-start.5 = (bf16[8,16,512]{2,1,0:T(8,128)(2,1)S(1)}, bf16[8,16,512]{2,1,0:T(8,128)(2,1)S(1)}, u32[]{:S(2)}, u32[]{:S(2)}) collective-permute-start(bf16[8,16,512]{2,1,0:T(8,128)(2,1)S(1)} %get-tuple-element.90), channel_id=1, source_target_pairs={{4,0},{8,4},{12,8},{16,12},{20,16},{24,20},{28,24},{5,1},{9,5},{13... | collective-permute-start | bytes 393224 | tf_op jit(solution)/shard_map/ppermute | solution.py:23
  25.0 21.8 %copy-start.63 = (pred[2,2]{1,0:T(4,128)(4,1)}, pred[2,2]{1,0:T(4,128)(4,1)S(1)}, u32[]{:S(2)}) copy-start(pred[2,2]{1,0:T(4,128)(4,1)S(1)} %get-tuple-element.122) | copy-start | bytes 16
  25.1 22.6 %copy-start.61 = (pred[2,2]{1,0:T(4,128)(4,1)}, pred[2,2]{1,0:T(4,128)(4,1)S(1)}, u32[]{:S(2)}) copy-start(pred[2,2]{1,0:T(4,128)(4,1)S(1)} %get-tuple-element.115) | copy-start | bytes 16
  25.1 23.4 %copy-start.77 = (pred[2,2]{1,0:T(4,128)(4,1)}, pred[2,2]{1,0:T(4,128)(4,1)S(1)}, u32[]{:S(2)}) copy-start(pred[2,2]{1,0:T(4,128)(4,1)S(1)} %get-tuple-element.123) | copy-start | bytes 16
  25.1 24.3 %copy-start.67 = (pred[2,2]{1,0:T(4,128)(4,1)}, pred[2,2]{1,0:T(4,128)(4,1)S(1)}, u32[]{:S(2)}) copy-start(pred[2,2]{1,0:T(4,128)(4,1)S(1)} %get-tuple-element.120) | copy-start | bytes 16
  30.2 9.3 %collective-permute-start.6 = (bf16[32,8,512]{2,1,0:T(8,128)(2,1)S(1)}, bf16[32,8,512]{2,1,0:T(8,128)(2,1)S(1)}, u32[]{:S(2)}, u32[]{:S(2)}) collective-permute-start(bf16[32,8,512]{2,1,0:T(8,128)(2,1)S(1)} %get-tuple-element.83), channel_id=1, source_target_pairs={{0,1},{1,2},{2,3},{4,5},{5,6},{6,7},{8,9},{9,10},{10,11},{12,13},{... | collective-permute-start | bytes 786440 | tf_op jit(solution)/shard_map/ppermute | solution.py:20
  31.5 8.0 %collective-permute-start.7 = (bf16[32,8,512]{2,1,0:T(8,128)(2,1)S(1)}, bf16[32,8,512]{2,1,0:T(8,128)(2,1)S(1)}, u32[]{:S(2)}, u32[]{:S(2)}) collective-permute-start(bf16[32,8,512]{2,1,0:T(8,128)(2,1)S(1)} %get-tuple-element.84), channel_id=1, source_target_pairs={{1,0},{2,1},{3,2},{5,4},{6,5},{7,6},{9,8},{10,9},{11,10},{13,12},{... | collective-permute-start | bytes 786440 | tf_op jit(solution)/shard_map/ppermute | solution.py:23
  33.0 6.8 %collective-permute-start.2 = (bf16[32,8,512]{2,1,0:T(8,128)(2,1)S(1)}, bf16[32,8,512]{2,1,0:T(8,128)(2,1)S(1)}, u32[]{:S(2)}, u32[]{:S(2)}) collective-permute-start(bf16[32,8,512]{2,1,0:T(8,128)(2,1)S(1)} %get-tuple-element.87), channel_id=1, source_target_pairs={{0,1},{1,2},{2,3},{4,5},{5,6},{6,7},{8,9},{9,10},{10,11},{12,13},{... | collective-permute-start | bytes 786440 | tf_op jit(solution)/shard_map/ppermute | solution.py:20
  37.7 4.8 %collective-permute-start.3 = (bf16[32,8,512]{2,1,0:T(8,128)(2,1)S(1)}, bf16[32,8,512]{2,1,0:T(8,128)(2,1)}, u32[]{:S(2)}, u32[]{:S(2)}) collective-permute-start(bf16[32,8,512]{2,1,0:T(8,128)(2,1)S(1)} %get-tuple-element.88), channel_id=1, source_target_pairs={{1,0},{2,1},{3,2},{5,4},{6,5},{7,6},{9,8},{10,9},{11,10},{13,12},{... | collective-permute-start | bytes 786440 | tf_op jit(solution)/shard_map/ppermute | solution.py:23
  88.7 5.5 %collective-permute-start.8 = (f32[8,16,4]{1,0,2:T(8,128)S(1)}, f32[8,16,4]{1,0,2:T(8,128)S(1)}, u32[]{:S(2)}, u32[]{:S(2)}) collective-permute-start(f32[8,16,4]{1,0,2:T(8,128)S(1)} %slice.401), channel_id=1, source_target_pairs={{0,4},{4,8},{8,12},{12,16},{16,20},{20,24},{24,28},{1,5},{5,9},{9,... | collective-permute-start | bytes 6152 | tf_op jit(solution)/shard_map/ppermute | solution.py:20
  93.0 6.0 %collective-permute-start.9 = (f32[8,16,4]{1,0,2:T(8,128)S(1)}, f32[8,16,4]{1,0,2:T(8,128)S(1)}, u32[]{:S(2)}, u32[]{:S(2)}) collective-permute-start(f32[8,16,4]{1,0,2:T(8,128)S(1)} %slice.403), channel_id=1, source_target_pairs={{4,0},{8,4},{12,8},{16,12},{20,16},{24,20},{28,24},{5,1},{9,5},{13... | collective-permute-start | bytes 6152 | tf_op jit(solution)/shard_map/ppermute | solution.py:23
  99.1 3.7 %collective-permute-start.10 = (f32[32,8,4]{1,0,2:T(8,128)S(1)}, f32[32,8,4]{1,0,2:T(8,128)S(1)}, u32[]{:S(2)}, u32[]{:S(2)}) collective-permute-start(f32[32,8,4]{1,0,2:T(8,128)S(1)} %get-tuple-element.93), channel_id=1, source_target_pairs={{0,1},{1,2},{2,3},{4,5},{5,6},{6,7},{8,9},{9,10},{10,11},{12,13},{... | collective-permute-start | bytes 12296 | tf_op jit(solution)/shard_map/ppermute | solution.py:20
  100.4 4.9 %collective-permute-start.11 = (f32[32,8,4]{1,0,2:T(8,128)S(1)}, f32[32,8,4]{1,0,2:T(8,128)S(1)}, u32[]{:S(2)}, u32[]{:S(2)}) collective-permute-start(f32[32,8,4]{1,0,2:T(8,128)S(1)} %get-tuple-element.94), channel_id=1, source_target_pairs={{1,0},{2,1},{3,2},{5,4},{6,5},{7,6},{9,8},{10,9},{11,10},{13,12},{... | collective-permute-start | bytes 12296 | tf_op jit(solution)/shard_map/ppermute | solution.py:23
  123.3 40.5 %copy-start.25 = (bf16[256,256]{1,0:T(8,128)(2,1)S(1)}, bf16[256,256]{1,0:T(8,128)(2,1)}, u32[]{:S(2)}) copy-start(bf16[256,256]{1,0:T(8,128)(2,1)} %param.13) | copy-start | bytes 393220
  123.4 41.2 %copy-start.51 = (bf16[2,8,2,8,256]{4,3,2,1,0:T(8,128)(2,1)S(1)}, bf16[2,8,2,8,256]{4,3,2,1,0:T(8,128)(2,1)}, u32[]{:S(2)}) copy-start(bf16[2,8,2,8,256]{4,3,2,1,0:T(8,128)(2,1)} %copy-done.50) | copy-start | bytes 393220
  123.4 41.2 %copy-start.56 = (bf16[256,256]{1,0:T(8,128)(2,1)S(1)}, bf16[256,256]{1,0:T(8,128)(2,1)}, u32[]{:S(2)}) copy-start(bf16[256,256]{1,0:T(8,128)(2,1)} %param.12) | copy-start | bytes 393220
  123.4 41.2 %copy-start.57 = (bf16[256,256]{1,0:T(8,128)(2,1)S(1)}, bf16[256,256]{1,0:T(8,128)(2,1)}, u32[]{:S(2)}) copy-start(bf16[256,256]{1,0:T(8,128)(2,1)} %param.11) | copy-start | bytes 393220
  123.5 41.2 %copy-start.58 = (bf16[256,256]{1,0:T(8,128)(2,1)S(1)}, bf16[256,256]{1,0:T(8,128)(2,1)}, u32[]{:S(2)}) copy-start(bf16[256,256]{1,0:T(8,128)(2,1)} %param.10) | copy-start | bytes 393220
  125.5 122.0 %all-reduce.5.cloned.1.call-start = ((), (), s32[]{:S(2)}) async-start(), calls=%async_computation.1 | async-start | bytes 2097152 | tf_op jit(solution)/shard_map/psum | solution.py:175
  (70 other events, 381.4 us)
Sparse Core Ops, SparseCore 0:
  10.2 55.1 all-gather.2
  125.6 38.1 all-reduce.6
  168.1 79.3 all-reduce.4
